TPU v7x, 32 devices: a whole 2x2x4 slice. The times are simulated.
32 devices in a mesh: rows: 8 (over z, x), cols: 4 (over y, core).
Axes of the slice: x: 2, y: 2, z: 4, core: 2. Of those that a mesh axis runs over, the one named last changes fastest.
Arguments:
- vectors: bfloat16 [64, 131072], P('cols', 'rows'), may hold values from -110 to 110
- tile_vals: bfloat16 [1536, 256, 256], P('rows'), may hold values from -0.21875 to 0.21875
- tile_row: int32 [8, 192], P('rows'), may hold values from 0 to 63
- tile_src: int32 [8, 192], P('rows'), may hold values from 0 to 191, each once within a row
- send_list: int32 [64, 16], P('rows'), may hold values from 0 to 63
- ritz_matrix: bfloat16 [64, 64], P(None, 'cols'), may hold values from -0.75 to 0.75
Outputs:
- rotated: bfloat16 [64, 131072], P('cols', 'rows')
- gram_matrix: float32 [64, 64], P('cols')
- projected: float32 [64, 64], P('cols')
Inputs may be any that keep to these rules, and one draw needn't show every extreme that they name: Each row of tile_src holds every number once, so that each own or received block is read by exactly one tile.
All inputs are finite; a program needn't handle non-finite values.
Results may differ from a plain program's by a relative error of at most 0.0062.
Values may be sent and summed in bfloat16 or wider, within the bound.
No kernel may reach another device: no remote copies, remote signals or barrier semaphores. Data moves between devices by JAX's collectives and lax.ppermute only.
A program may use at most 128 MiB of HBM per device.

v0:
```python
import jax
import jax.numpy as jnp
from jax import lax
from jax.sharding import PartitionSpec as P


def tile_products(sources, tile_block, row_ids, src_ids, nblocks):
    chosen = jnp.take(sources, src_ids, axis=1)
    products = jnp.einsum("ktc,trc->ktr", chosen, tile_block, preferred_element_type=jnp.float32)
    onehot = (row_ids[None, :] == jnp.arange(nblocks, dtype=jnp.int32)[:, None]).astype(jnp.float32)
    summed = jnp.einsum("bt,ktr->kbr", onehot, products, precision=lax.Precision.HIGHEST)
    return summed.reshape(summed.shape[0], -1)


def apply_operator(vectors, tile_vals, tile_row, tile_src, send_list):
    columns, length = vectors.shape
    tile_side = tile_vals.shape[1]
    nblocks = length // tile_side
    blocked = vectors.reshape(columns, nblocks, tile_side)
    outgoing = jnp.take(blocked, send_list.reshape(-1), axis=1)
    incoming = lax.all_to_all(outgoing, "rows", split_axis=1, concat_axis=1, tiled=True)
    row_ids = tile_row.reshape(-1)
    src_ids = tile_src.reshape(-1)
    sources = jnp.concatenate([blocked, incoming], axis=1)
    return tile_products(sources, tile_vals, row_ids, src_ids, nblocks)


def contract_nodes(left_side, right_side):
    return lax.dot_general(
        left_side, right_side, (((1,), (1,)), ((), ())), preferred_element_type=jnp.float32
    )


def body(vectors, tile_vals, tile_row, tile_src, send_list, ritz_matrix):
    first_pass = apply_operator(vectors, tile_vals, tile_row, tile_src, send_list).astype(
        jnp.bfloat16
    )
    second = apply_operator(first_pass, tile_vals, tile_row, tile_src, send_list)
    filtered = (2.0 * second - vectors.astype(jnp.float32)).astype(jnp.bfloat16)
    total_nodes = vectors.shape[1] * lax.axis_size("rows")
    operated = apply_operator(filtered, tile_vals, tile_row, tile_src, send_list).astype(
        jnp.bfloat16
    )
    portion = lax.all_gather(filtered, "cols", axis=0, tiled=True)
    gram_piece = contract_nodes(filtered, portion)
    proj_piece = contract_nodes(operated, portion)
    turned = lax.dot_general(
        ritz_matrix, portion, (((0,), (0,)), ((), ())), preferred_element_type=jnp.float32
    )
    gram_total, proj_total = lax.psum((gram_piece, proj_piece), "rows")
    gram_matrix = gram_total / total_nodes
    projected = proj_total / total_nodes
    rotated = turned.astype(jnp.bfloat16)
    return (rotated, gram_matrix, projected)


def solution(mesh):
    return jax.shard_map(
        body,
        mesh=mesh,
        in_specs=(
            P("cols", "rows"),
            P("rows", None, None),
            P("rows", None),
            P("rows", None),
            P("rows", None),
            P(None, "cols"),
        ),
        out_specs=(P("cols", "rows"), P("cols", None), P("cols", None)),
        check_vma=False,
    )
```

profile of v0, /device:TPU:0, one launch (start us, length us, event | category | flops | bytes accessed | tf_op | source)
XLA Modules:
  0.0 207.6 jit_solution(13215640300237485455)
XLA Ops:
  7.2 0.8 reshape.40
  8.0 1.1 copy.41
  9.7 1.2 select_bitcast_fusion.2
  10.9 7.4 %all-to-all-start = ((bf16[16,128,256]{2,0,1:T(8,128)(2,1)}), bf16[16,128,256]{2,0,1:T(8,128)(2,1)S(1)}, u32[]{:S(2)}, u32[]{:S(2)}) async-start(bf16[16,128,256]{2,0,1:T(8,128)(2,1)} %select_bitcast_fusion.2), calls=%async_computation | async-start | bytes 2097152 | tf_op jit(solution)/shard_map/all_to_all | solution.py:21
  18.4 25.7 %all-to-all-done = bf16[16,128,256]{2,0,1:T(8,128)(2,1)S(1)} async-done(((bf16[16,128,256]{2,0,1:T(8,128)(2,1)}), bf16[16,128,256]{2,0,1:T(8,128)(2,1)S(1)}, u32[]{:S(2)}, u32[]{:S(2)}) %all-to-all-start) | async-done | bytes 1048608 | tf_op jit(solution)/shard_map/all_to_all | solution.py:21
  44.2 2.0 gather_fusion.1
  46.3 12.0 %convolution_bitcast_fusion.2 = f32[16,192,256]{2,0,1:T(8,128)S(1)} fusion(bf16[192,256,256]{2,1,0:T(8,128)(2,1)} %param.11, bf16[192,16,256]{2,1,0:T(8,128)(2,1)} %gather_fusion.1, pred[192]{0:T(512)(128)(4,1)S(1)} %compare_and_fusion), kind=kOutput, calls=%fused_computation.16 | convolution fusion | flops 403439616 | bytes 29884608 | tf_op jit(solution)/shard_map/ktc,trc->ktr/dot_general | solution.py:9
  58.3 3.2 %fusion.25 = bf16[16,64,256]{2,1,0:T(8,128)(2,1)S(1)} fusion(f32[16,192,256]{2,0,1:T(8,128)S(1)} %convolution_bitcast_fusion.2, s32[192]{0:T(256)S(1)} %bitcast.65), kind=kOutput, calls=%fused_computation.32 | convolution fusion | flops 604254208 | bytes 3670784 | tf_op jit(solution)/shard_map/bt,ktr->kbr/dot_general | solution.py:11
  62.6 29.3 %all_to_all.15 = bf16[16,128,256]{2,0,1:T(8,128)(2,1)S(1)} all-to-all(bf16[16,128,256]{2,0,1:T(8,128)(2,1)S(1)} %select_bitcast_fusion.1), channel_id=1, replica_groups=mesh['rows'=8,'cols'=4] {'rows'}, dimensions={1} | all-to-all | bytes 2097152 | tf_op jit(solution)/shard_map/all_to_all | solution.py:21
  92.1 2.0 gather_fusion.3
  94.1 12.0 %convolution_bitcast_fusion.1 = f32[16,192,256]{2,0,1:T(8,128)S(1)} fusion(bf16[192,256,256]{2,1,0:T(8,128)(2,1)} %param.11, bf16[192,16,256]{2,1,0:T(8,128)(2,1)} %gather_fusion.3, pred[192]{0:T(512)(128)(4,1)S(1)} %compare_and_fusion), kind=kOutput, calls=%fused_computation.15 | convolution fusion | flops 403439616 | bytes 29884608 | tf_op jit(solution)/shard_map/ktc,trc->ktr/dot_general | solution.py:9
  106.1 3.2 %fusion.16 = f32[16,256,64]{1,2,0:T(8,128)S(1)} fusion(f32[16,192,256]{2,0,1:T(8,128)S(1)} %convolution_bitcast_fusion.1, s32[192]{0:T(256)S(1)} %bitcast.66), kind=kOutput, calls=%fused_computation.29 | convolution fusion | flops 604254208 | bytes 4195072 | tf_op jit(solution)/shard_map/bt,ktr->kbr/dot_general | solution.py:11
  110.5 0.6 gather_fusion.4
  111.2 1.2 select_bitcast_fusion
  112.4 4.2 %all-to-all-start.2 = ((bf16[16,128,256]{2,0,1:T(8,128)(2,1)}), bf16[16,128,256]{2,0,1:T(8,128)(2,1)}, u32[]{:S(2)}, u32[]{:S(2)}) async-start(bf16[16,128,256]{2,0,1:T(8,128)(2,1)} %select_bitcast_fusion), calls=%async_computation.2 | async-start | bytes 2097152 | tf_op jit(solution)/shard_map/all_to_all | solution.py:21
  117.4 24.4 %all-to-all-done.2 = bf16[16,128,256]{2,0,1:T(8,128)(2,1)} async-done(((bf16[16,128,256]{2,0,1:T(8,128)(2,1)}), bf16[16,128,256]{2,0,1:T(8,128)(2,1)}, u32[]{:S(2)}, u32[]{:S(2)}) %all-to-all-start.2) | async-done | bytes 1048608 | tf_op jit(solution)/shard_map/all_to_all | solution.py:21
  141.8 1.4 pad_maximum_fusion.2
  143.2 2.0 gather_fusion.5
  145.2 12.0 %convolution_bitcast_fusion = f32[16,192,256]{2,0,1:T(8,128)S(1)} fusion(bf16[192,256,256]{2,1,0:T(8,128)(2,1)} %param.11, bf16[192,16,256]{2,1,0:T(8,128)(2,1)} %gather_fusion.5, pred[192]{0:T(512)(128)(4,1)S(1)} %compare_and_fusion), kind=kOutput, calls=%fused_computation.14 | convolution fusion | flops 403439616 | bytes 29884608 | tf_op jit(solution)/shard_map/ktc,trc->ktr/dot_general | solution.py:9
  157.2 3.2 %fusion.22 = bf16[16,256,64]{1,2,0:T(8,128)(2,1)S(1)} fusion(f32[16,192,256]{2,0,1:T(8,128)S(1)} %convolution_bitcast_fusion, s32[192]{0:T(256)S(1)} %bitcast.67), kind=kOutput, calls=%fused_computation.31 | convolution fusion | flops 604254208 | bytes 3670784 | tf_op jit(solution)/shard_map/bt,ktr->kbr/dot_general | solution.py:11
  160.7 2.5 %fusion.41 = f32[16,64]{1,0:T(8,128)S(1)} fusion(bf16[16,16384]{1,0:T(8,128)(2,1)} %copy-done.2, bf16[64,16384]{1,0:T(8,128)(2,1)} %all-gather.2.cloned.1.call-done), kind=kOutput, calls=%fused_computation.58 | convolution fusion | flops 33554432 | bytes 2625536 | tf_op jit(solution)/shard_map/dot_general | solution.py:29
  163.3 0.7 fusion.42
  163.9 35.0 %all-reduce = (f32[16,64]{1,0:T(8,128)S(1)}, f32[16,64]{1,0:T(8,128)S(1)}) all-reduce(f32[16,64]{1,0:T(8,128)S(1)} %fusion.41, f32[16,64]{1,0:T(8,128)S(1)} %fusion.42), channel_id=1, replica_groups=mesh['rows'=8,'cols'=4] {'rows'}, use_global_device_ids=true, to_apply=%region_0.3 | all-reduce | flops 2048 | bytes 16384 | tf_op jit(solution)/shard_map/psum | solution.py:50
  199.5 1.2 fusion
  (32 shorter events, 5.0 us)
Async XLA Ops:
  7.2 192.4 %copy-start = (bf16[64,16]{0,1:T(8,128)(2,1)S(1)}, bf16[64,16]{0,1:T(8,128)(2,1)}, u32[]{:S(2)}) copy-start(bf16[64,16]{0,1:T(8,128)(2,1)} %param.15) | copy-start | bytes 6148
  10.9 7.4 %copy-start.5 = (s32[1,192]{1,0:T(1,128)S(1)}, s32[1,192]{1,0:T(1,128)}, u32[]{:S(2)}) copy-start(s32[1,192]{1,0:T(1,128)} %param.13) | copy-start | bytes 2308
  10.9 33.2 %all-to-all-start = ((bf16[16,128,256]{2,0,1:T(8,128)(2,1)}), bf16[16,128,256]{2,0,1:T(8,128)(2,1)S(1)}, u32[]{:S(2)}, u32[]{:S(2)}) async-start(bf16[16,128,256]{2,0,1:T(8,128)(2,1)} %select_bitcast_fusion.2), calls=%async_computation | async-start | bytes 2097152 | tf_op jit(solution)/shard_map/all_to_all | solution.py:21
  46.3 12.1 %copy-start.4 = (s32[1,192]{1,0:T(1,128)S(1)}, s32[1,192]{1,0:T(1,128)}, u32[]{:S(2)}) copy-start(s32[1,192]{1,0:T(1,128)} %param.12) | copy-start | bytes 2308
  109.3 1.0 copy-start.3
  110.4 0.8 copy-start.2
  112.4 29.4 %all-to-all-start.2 = ((bf16[16,128,256]{2,0,1:T(8,128)(2,1)}), bf16[16,128,256]{2,0,1:T(8,128)(2,1)}, u32[]{:S(2)}, u32[]{:S(2)}) async-start(bf16[16,128,256]{2,0,1:T(8,128)(2,1)} %select_bitcast_fusion), calls=%async_computation.2 | async-start | bytes 2097152 | tf_op jit(solution)/shard_map/all_to_all | solution.py:21
  116.7 44.0 %all-gather.2.cloned.1.call-start = ((), (), s32[]{:S(2)}) async-start(), calls=%async_computation.3 | async-start | bytes 2621440 | tf_op jit(solution)/shard_map/all_gather | solution.py:44
  160.7 2.6 %copy-start.1 = (bf16[64,16384]{1,0:T(8,128)(2,1)S(1)}, bf16[64,16384]{1,0:T(8,128)(2,1)}, u32[]{:S(2)}) copy-start(bf16[64,16384]{1,0:T(8,128)(2,1)} %all-gather.2.cloned.1.call-done) | copy-start | bytes 6291460
Sparse Core Ops, SparseCore 0:
  119.6 23.8 all-gather.1
where the time goes:
time: 208 us
  blocking collectives  64.2 us (31%)
  waiting for transfers between devices  50.6 us (24%)
  matrix products  50 us (24%)
  between operations  14.2 us (7%)
  starting transfers between devices  11.9 us (6%)
  local copies, waits for them, and re-layouts  11.7 us (6%)
  other arithmetic  4.96 us (2%)
    all_to_all x2, waiting for transfers between devices, apply_operator(): lax.all_to_all(outgoing, 'rows', split_axis=1, concat_axis=1, tiled=True)  50.1 us
    dot_general x3, matrix products, tile_products(): jnp.einsum('ktc,trc->ktr', chosen, tile_block, preferred_element_type=jnp...  36.1 us
    psum x1, blocking collectives, body(): gram_total, proj_total = lax.psum((gram_piece, proj_piece), 'rows')  35 us
    all_to_all x1, blocking collectives, apply_operator(): lax.all_to_all(outgoing, 'rows', split_axis=1, concat_axis=1, tiled=True)  29.3 us
    all_to_all x2, starting transfers between devices, apply_operator(): lax.all_to_all(outgoing, 'rows', split_axis=1, concat_axis=1, tiled=True)  11.6 us
    dot_general x3, matrix products, tile_products(): jnp.einsum('bt,ktr->kbr', onehot, products, precision=lax.Precision.HIGHEST)  9.49 us
    gather x3, local copies, waits for them, and re-layouts, tile_products(): chosen = jnp.take(sources, src_ids, axis=1)  6.1 us
  transfers between devices with their start and end apart: 3, of which 2 were waited for; matrix products, arithmetic and copies ran while one was open for 9% of the time, Pallas kernels for 0%

commit v1 on v0

--- a/solution.py
+++ b/solution.py
@@ -18,7 +18,10 @@
     nblocks = length // tile_side
     blocked = vectors.reshape(columns, nblocks, tile_side)
     outgoing = jnp.take(blocked, send_list.reshape(-1), axis=1)
-    incoming = lax.all_to_all(outgoing, "rows", split_axis=1, concat_axis=1, tiled=True)
+    clean = jax.lax.all_to_all(
+        jnp.stack(jnp.split(outgoing, jax.lax.axis_size("rows"), 1), 0), "rows", 0, 0
+    )
+    incoming = jnp.concatenate(clean, 1)
     row_ids = tile_row.reshape(-1)
     src_ids = tile_src.reshape(-1)
     sources = jnp.concatenate([blocked, incoming], axis=1)

time: 208 us -> 217 us (1.043)
  local copies, waits for them, and re-layouts: 11.7 us -> 23.2 us
    unnamed x14 -> x37, local copies, waits for them, and re-layouts: 1.45 us -> 11.7 us
where the time goes in v1:
time: 217 us
  blocking collectives  64.3 us (30%)
  waiting for transfers between devices  51 us (24%)
  matrix products  50 us (23%)
  local copies, waits for them, and re-layouts  23.2 us (11%)
  between operations  14.3 us (7%)
  starting transfers between devices  11.2 us (5%)
  other arithmetic  2.98 us (1%)
    all_to_all x2, waiting for transfers between devices, apply_operator(): jax.lax.all_to_all(jnp.stack(jnp.split(outgoing, jax.lax.axis_size('rows'...  50.6 us
    dot_general x3, matrix products, tile_products(): jnp.einsum('ktc,trc->ktr', chosen, tile_block, preferred_element_type=jnp...  36.1 us
    psum x1, blocking collectives, body(): gram_total, proj_total = lax.psum((gram_piece, proj_piece), 'rows')  35.1 us
    all_to_all x1, blocking collectives, apply_operator(): jax.lax.all_to_all(jnp.stack(jnp.split(outgoing, jax.lax.axis_size('rows'...  29.3 us
    unnamed x37, local copies, waits for them, and re-layouts  11.7 us
    all_to_all x2, starting transfers between devices, apply_operator(): jax.lax.all_to_all(jnp.stack(jnp.split(outgoing, jax.lax.axis_size('rows'...  10.9 us
    dot_general x3, matrix products, tile_products(): jnp.einsum('bt,ktr->kbr', onehot, products, precision=lax.Precision.HIGHEST)  9.48 us
    gather x3, local copies, waits for them, and re-layouts, tile_products(): chosen = jnp.take(sources, src_ids, axis=1)  6.1 us
  transfers between devices with their start and end apart: 3, of which 2 were waited for; matrix products, arithmetic and copies ran while one was open for 9% of the time, Pallas kernels for 0%

profile of v1, /device:TPU:0, one launch (start us, length us, event | category | flops | bytes accessed | tf_op | source)
XLA Modules:
  0.0 217.0 jit_solution(14044400899951771982)
XLA Ops:
  7.2 0.8 reshape.58
  8.0 1.1 copy.56
  13.2 0.7 fusion.49
  13.9 0.7 fusion.48
  15.2 7.3 %all-to-all-start = ((bf16[8,16,16,256]{3,1,2,0:T(8,128)(2,1)}), bf16[8,16,16,256]{3,1,2,0:T(8,128)(2,1)S(1)}, u32[]{:S(2)}, u32[]{:S(2)}) async-start(bf16[8,16,16,256]{3,1,2,0:T(8,128)(2,1)} %fusion.47), calls=%async_computation | async-start | bytes 2097152 | tf_op jit(solution)/shard_map/all_to_all | solution.py:21
  22.5 25.7 %all-to-all-done = bf16[8,16,16,256]{3,1,2,0:T(8,128)(2,1)S(1)} async-done(((bf16[8,16,16,256]{3,1,2,0:T(8,128)(2,1)}), bf16[8,16,16,256]{3,1,2,0:T(8,128)(2,1)S(1)}, u32[]{:S(2)}, u32[]{:S(2)}) %all-to-all-start) | async-done | bytes 1048608 | tf_op jit(solution)/shard_map/all_to_all | solution.py:21
  48.4 2.0 gather_fusion.1
  50.4 12.0 %convolution_bitcast_fusion.2 = f32[16,192,256]{2,0,1:T(8,128)S(1)} fusion(bf16[192,256,256]{2,1,0:T(8,128)(2,1)} %param.11, bf16[192,16,256]{2,1,0:T(8,128)(2,1)} %gather_fusion.1, pred[192]{0:T(512)(128)(4,1)S(1)} %compare_and_fusion), kind=kOutput, calls=%fused_computation.16 | convolution fusion | flops 403439616 | bytes 29884608 | tf_op jit(solution)/shard_map/ktc,trc->ktr/dot_general | solution.py:9
  62.5 3.2 %fusion.25 = bf16[16,64,256]{2,1,0:T(8,128)(2,1)S(1)} fusion(f32[16,192,256]{2,0,1:T(8,128)S(1)} %convolution_bitcast_fusion.2, s32[192]{0:T(256)S(1)} %bitcast.173), kind=kOutput, calls=%fused_computation.32 | convolution fusion | flops 604254208 | bytes 3670784 | tf_op jit(solution)/shard_map/bt,ktr->kbr/dot_general | solution.py:11
  66.9 29.3 %all_to_all.15 = bf16[8,16,16,256]{3,1,2,0:T(8,128)(2,1)S(1)} all-to-all(bf16[8,16,16,256]{3,1,2,0:T(8,128)(2,1)S(1)} %fusion.39), channel_id=1, replica_groups=mesh['rows'=8,'cols'=4] {'rows'}, dimensions={0} | all-to-all | bytes 2097152 | tf_op jit(solution)/shard_map/all_to_all | solution.py:21
  96.4 2.0 gather_fusion.3
  98.4 12.0 %convolution_bitcast_fusion.1 = f32[16,192,256]{2,0,1:T(8,128)S(1)} fusion(bf16[192,256,256]{2,1,0:T(8,128)(2,1)} %param.11, bf16[192,16,256]{2,1,0:T(8,128)(2,1)} %gather_fusion.3, pred[192]{0:T(512)(128)(4,1)S(1)} %compare_and_fusion), kind=kOutput, calls=%fused_computation.15 | convolution fusion | flops 403439616 | bytes 29884608 | tf_op jit(solution)/shard_map/ktc,trc->ktr/dot_general | solution.py:9
  110.4 3.2 %fusion.16 = f32[16,256,64]{1,2,0:T(8,128)S(1)} fusion(f32[16,192,256]{2,0,1:T(8,128)S(1)} %convolution_bitcast_fusion.1, s32[192]{0:T(256)S(1)} %bitcast.174), kind=kOutput, calls=%fused_computation.29 | convolution fusion | flops 604254208 | bytes 4195072 | tf_op jit(solution)/shard_map/bt,ktr->kbr/dot_general | solution.py:11
  119.0 0.7 fusion.33
  121.0 3.6 %all-to-all-start.2 = ((bf16[8,16,16,256]{3,1,2,0:T(8,128)(2,1)}), bf16[8,16,16,256]{3,1,2,0:T(8,128)(2,1)S(1)}, u32[]{:S(2)}, u32[]{:S(2)}) async-start(bf16[8,16,16,256]{3,1,2,0:T(8,128)(2,1)} %fusion.31), calls=%async_computation.2 | async-start | bytes 2097152 | tf_op jit(solution)/shard_map/all_to_all | solution.py:21
  125.4 24.8 %all-to-all-done.2 = bf16[8,16,16,256]{3,1,2,0:T(8,128)(2,1)S(1)} async-done(((bf16[8,16,16,256]{3,1,2,0:T(8,128)(2,1)}), bf16[8,16,16,256]{3,1,2,0:T(8,128)(2,1)S(1)}, u32[]{:S(2)}, u32[]{:S(2)}) %all-to-all-start.2) | async-done | bytes 1048608 | tf_op jit(solution)/shard_map/all_to_all | solution.py:21
  150.2 1.0 copy-done.3
  151.2 1.4 pad_maximum_fusion.2
  152.5 2.0 gather_fusion.5
  154.6 12.0 %convolution_bitcast_fusion = f32[16,192,256]{2,0,1:T(8,128)S(1)} fusion(bf16[192,256,256]{2,1,0:T(8,128)(2,1)} %param.11, bf16[192,16,256]{2,1,0:T(8,128)(2,1)} %gather_fusion.5, pred[192]{0:T(512)(128)(4,1)S(1)} %compare_and_fusion), kind=kOutput, calls=%fused_computation.14 | convolution fusion | flops 403439616 | bytes 29884608 | tf_op jit(solution)/shard_map/ktc,trc->ktr/dot_general | solution.py:9
  166.6 3.2 %fusion.22 = bf16[16,256,64]{1,2,0:T(8,128)(2,1)S(1)} fusion(f32[16,192,256]{2,0,1:T(8,128)S(1)} %convolution_bitcast_fusion, s32[192]{0:T(256)S(1)} %bitcast.175), kind=kOutput, calls=%fused_computation.31 | convolution fusion | flops 604254208 | bytes 3670784 | tf_op jit(solution)/shard_map/bt,ktr->kbr/dot_general | solution.py:11
  170.1 2.5 %fusion.65 = f32[16,64]{1,0:T(8,128)S(1)} fusion(bf16[16,16384]{1,0:T(8,128)(2,1)} %copy-done.2, bf16[64,16384]{1,0:T(8,128)(2,1)} %all-gather.2.cloned.1.call-done), kind=kOutput, calls=%fused_computation.106 | convolution fusion | flops 33554432 | bytes 2625536 | tf_op jit(solution)/shard_map/dot_general | solution.py:32
  173.3 35.1 %all-reduce = (f32[16,64]{1,0:T(8,128)S(1)}, f32[16,64]{1,0:T(8,128)S(1)}) all-reduce(f32[16,64]{1,0:T(8,128)S(1)} %fusion.65, f32[16,64]{1,0:T(8,128)S(1)} %fusion.66), channel_id=1, replica_groups=mesh['rows'=8,'cols'=4] {'rows'}, use_global_device_ids=true, to_apply=%region_0.3 | all-reduce | flops 2048 | bytes 16384 | tf_op jit(solution)/shard_map/psum | solution.py:53
  209.0 1.2 fusion
  (58 shorter events, 15.3 us)
Async XLA Ops:
  7.2 201.8 %copy-start = (bf16[64,16]{0,1:T(8,128)(2,1)S(1)}, bf16[64,16]{0,1:T(8,128)(2,1)}, u32[]{:S(2)}) copy-start(bf16[64,16]{0,1:T(8,128)(2,1)} %param.15) | copy-start | bytes 6148
  12.6 9.9 %copy-start.6 = (s32[1,192]{1,0:T(1,128)S(1)}, s32[1,192]{1,0:T(1,128)}, u32[]{:S(2)}) copy-start(s32[1,192]{1,0:T(1,128)} %param.13) | copy-start | bytes 2308
  15.2 33.0 %all-to-all-start = ((bf16[8,16,16,256]{3,1,2,0:T(8,128)(2,1)}), bf16[8,16,16,256]{3,1,2,0:T(8,128)(2,1)S(1)}, u32[]{:S(2)}, u32[]{:S(2)}) async-start(bf16[8,16,16,256]{3,1,2,0:T(8,128)(2,1)} %fusion.47), calls=%async_computation | async-start | bytes 2097152 | tf_op jit(solution)/shard_map/all_to_all | solution.py:21
  50.4 12.1 %copy-start.5 = (s32[1,192]{1,0:T(1,128)S(1)}, s32[1,192]{1,0:T(1,128)}, u32[]{:S(2)}) copy-start(s32[1,192]{1,0:T(1,128)} %param.12) | copy-start | bytes 2308
  113.6 1.0 copy-start.4
  114.7 0.8 copy-start.2
  121.0 29.2 %all-to-all-start.2 = ((bf16[8,16,16,256]{3,1,2,0:T(8,128)(2,1)}), bf16[8,16,16,256]{3,1,2,0:T(8,128)(2,1)S(1)}, u32[]{:S(2)}, u32[]{:S(2)}) async-start(bf16[8,16,16,256]{3,1,2,0:T(8,128)(2,1)} %fusion.31), calls=%async_computation.2 | async-start | bytes 2097152 | tf_op jit(solution)/shard_map/all_to_all | solution.py:21
  124.6 45.5 %all-gather.2.cloned.1.call-start = ((), (), s32[]{:S(2)}) async-start(), calls=%async_computation.3 | async-start | bytes 2621440 | tf_op jit(solution)/shard_map/all_gather | solution.py:47
  150.2 1.0 copy-start.3
  170.1 2.6 %copy-start.1 = (bf16[64,16384]{1,0:T(8,128)(2,1)S(1)}, bf16[64,16384]{1,0:T(8,128)(2,1)}, u32[]{:S(2)}) copy-start(bf16[64,16384]{1,0:T(8,128)(2,1)} %all-gather.2.cloned.1.call-done) | copy-start | bytes 6291460
Sparse Core Ops, SparseCore 0:
  127.6 23.9 all-gather.1
